TPU v7x, 32 devices: a whole 2x2x4 slice. The times are simulated.
32 devices in a mesh: groups: 2 (over y), cent: 4 (over z), dp: 2 (over x), sub: 2 (over core).
Axes of the slice: x: 2, y: 2, z: 4, core: 2. Of those that a mesh axis runs over, the one named last changes fastest.
Arguments:
- embeddings: bfloat16 [1024, 768], P(('groups', 'cent', 'dp', 'sub')), parts along dimension 0, may hold values from -6 to 6
- weights: int32 [1024], P(('groups', 'cent', 'dp', 'sub')), parts along dimension 0, may hold values from 1 to 4
- centroids: bfloat16 [16384, 768], P(('groups', 'cent')), parts along dimension 0, may hold values from -6 to 6
- inverse_temp: float32 [1], replicated, may hold values from 16 to 256
Outputs:
- centroid_sums: float32 [16384, 768], P(('groups', 'cent', 'dp', 'sub')), parts along dimension 0
- renormed: bfloat16 [16384, 768], P(('groups', 'cent', 'dp', 'sub')), parts along dimension 0
- objective: float32 [1024], P(('groups', 'cent', 'dp', 'sub')), parts along dimension 0
There are 2 independent parts, one for each index of `groups`. A program takes and returns all parts, laid end to end along the dimension named above; an argument that names none is the same for every part. Nothing has to cross between parts.
All inputs are finite; a program needn't handle non-finite values.
Results may differ from a plain program's by a relative error of at most 0.0075.
The roundings to bfloat16 on the way count: a program that leaves them out, or rounds other values in their place, can miss the bound.
Values may be sent and summed in bfloat16 or wider, within the bound.
No kernel may reach another device: no remote copies, remote signals or barrier semaphores. Data moves between devices by JAX's collectives and lax.ppermute only.
A program may use at most 64 MiB of HBM per device.

v0:
```python
import jax
import jax.numpy as jnp
from jax import lax
from jax.sharding import PartitionSpec as P


def normalize(values):
    floats = values.astype(jnp.float32)
    return floats * lax.rsqrt(jnp.sum(floats * floats, axis=-1, keepdims=True) + 1e-06)


def shards(embeddings, weights, centroids, inverse_temp):
    sharpness = inverse_temp[0]
    unit_rows = normalize(embeddings).astype(jnp.bfloat16)
    unit_panel = normalize(centroids).astype(jnp.bfloat16)
    gathered_rows, gathered_weights = (
        lax.all_gather(unit_rows, "cent", axis=0, tiled=True),
        lax.all_gather(weights, "cent", axis=0, tiled=True),
    )
    scores = (
        lax.dot_general(
            gathered_rows, unit_panel, (((1,), (1,)), ((), ())), preferred_element_type=jnp.float32
        )
        * sharpness
    )
    local_peak = jnp.max(scores, axis=1)
    row_peak = lax.pmax(local_peak, "cent")
    row_total = lax.psum(jnp.sum(jnp.exp(scores - row_peak[:, None]), axis=1), "cent")
    log_sum = row_peak + jnp.log(row_total)
    weight_float = gathered_weights.astype(jnp.float32)
    responsibility = (weight_float[:, None] * jnp.exp(scores - log_sum[:, None])).astype(
        jnp.bfloat16
    )
    partial_value = lax.dot_general(
        responsibility, gathered_rows, (((0,), (0,)), ((), ())), preferred_element_type=jnp.float32
    ).astype(jnp.bfloat16)
    ones_row = jnp.ones((1, responsibility.shape[0]), jnp.bfloat16)
    weight_mass = jnp.dot(ones_row, responsibility, preferred_element_type=jnp.float32)[0].astype(
        jnp.bfloat16
    )
    own_count = centroids.shape[0] // lax.axis_size(("dp", "sub"))
    offset = lax.axis_index(("dp", "sub")) * own_count
    panel_sums, panel_mass = (
        lax.psum(partial_value, ("dp", "sub")).astype(jnp.float32),
        lax.psum(weight_mass, ("dp", "sub")).astype(jnp.float32),
    )
    centroid_sums = lax.dynamic_slice_in_dim(panel_sums, offset, own_count, 0)
    own_mass = lax.dynamic_slice_in_dim(panel_mass, offset, own_count, 0)
    own_cents = lax.dynamic_slice_in_dim(unit_panel, offset, own_count, 0).astype(jnp.float32)
    moved = own_cents + centroid_sums / (own_mass + 1.0)[:, None]
    renormed = normalize(moved).astype(jnp.bfloat16)
    row_offset = lax.axis_index("cent") * embeddings.shape[0]
    weighted_log_sum = weight_float * log_sum / sharpness
    objective = lax.dynamic_slice_in_dim(weighted_log_sum, row_offset, embeddings.shape[0], 0)
    return (centroid_sums, renormed, objective)


def solution(mesh):
    in_specs = (
        P(("groups", "cent", "dp", "sub"), None),
        P(("groups", "cent", "dp", "sub")),
        P(("groups", "cent"), None),
        P(),
    )
    out_specs = (
        P(("groups", "cent", "dp", "sub"), None),
        P(("groups", "cent", "dp", "sub"), None),
        P(("groups", "cent", "dp", "sub")),
    )
    return jax.shard_map(shards, mesh=mesh, in_specs=in_specs, out_specs=out_specs, check_vma=False)
```

profile of v0, /device:TPU:0, one launch (start us, length us, event | category | flops | bytes accessed | tf_op | source)
XLA Modules:
  0.0 144.0 jit_solution(1710212666322466163)
XLA Ops:
  7.2 0.0 copy-start.3
  7.2 0.0 all-reduce.3.cloned.1.call-start
  7.9 0.9 fusion.2
  8.8 1.2 dynamic-slice
  10.7 0.9 dynamic-update-slice
  11.6 9.9 %all-reduce = s32[128]{0:T(128)S(1)} all-reduce(s32[128]{0:T(128)S(1)} %dynamic-update-slice), channel_id=1, replica_groups=mesh['groups'=2,'cent'=4,'dp'=2,'sub'=2] {'cent'}, use_global_device_ids=true, to_apply=%add | all-reduce | flops 128 | bytes 1024
  21.5 0.0 copy-start
  21.5 2.7 %fusion = f32[2048]{0:T(1024)S(1)} fusion(bf16[2048,768]{1,0:T(8,128)(2,1)} %param.6), kind=kLoop, calls=%fused_computation.2 | loop fusion | flops 4716544 | bytes 3153920 | tf_op jit(solution)/shard_map/reduce_sum | solution.py:9
  24.2 0.0 copy-done.3
  24.2 0.1 fusion.3
  24.3 13.6 %all_gather.7 = bf16[128,768]{1,0:T(8,128)(2,1)S(1)} all-gather(bf16[32,768]{1,0:T(8,128)(2,1)S(1)} %fusion.3), channel_id=1, replica_groups=mesh['groups'=2,'cent'=4,'dp'=2,'sub'=2] {'cent'}, dimensions={0}, use_global_device_ids=true | all-gather | bytes 245760 | tf_op jit(solution)/shard_map/all_gather | solution.py:17
  37.9 0.0 copy-done
  37.9 0.6 fusion.1
  38.4 2.1 %fusion.7 = (f32[128]{0:T(128)S(1)}, f32[128,2048]{1,0:T(8,128)}) fusion(f32[]{:T(128)} %bitcast.8, bf16[128,768]{1,0:T(8,128)(2,1)S(1)} %all_gather.7, bf16[2048,768]{1,0:T(8,128)(2,1)S(1)} %fusion.1), kind=kOutput, calls=%fused_computation.25 | convolution fusion | flops 403177344 | bytes 4391428 | tf_op jit(solution)/shard_map/dot_general | solution.py:21
  40.6 10.4 %pmax.7 = f32[128]{0:T(128)S(1)} all-reduce(f32[128]{0:T(128)S(1)} %get-tuple-element.7), channel_id=1, replica_groups=mesh['groups'=2,'cent'=4,'dp'=2,'sub'=2] {'cent'}, use_global_device_ids=true, to_apply=%region_3.0 | all-reduce | flops 128 | bytes 1024 | tf_op jit(solution)/shard_map/pmax | solution.py:27
  51.0 1.5 %exponential_reduce_fusion = f32[128]{0:T(128)S(1)} fusion(f32[128,2048]{1,0:T(8,128)} %get-tuple-element.8, f32[128]{0:T(128)S(1)} %pmax.7), kind=kLoop, calls=%fused_computation.10 | loop fusion | flops 524160 | bytes 1049600 | tf_op jit(solution)/shard_map/reduce_sum | solution.py:28
  52.5 8.4 %psum.21 = f32[128]{0:T(128)S(1)} all-reduce(f32[128]{0:T(128)S(1)} %exponential_reduce_fusion), channel_id=1, replica_groups=mesh['groups'=2,'cent'=4,'dp'=2,'sub'=2] {'cent'}, use_global_device_ids=true, to_apply=%region_5.0 | all-reduce | flops 128 | bytes 1024 | tf_op jit(solution)/shard_map/psum | solution.py:28
  60.9 1.5 %multiply_convert_fusion.1 = bf16[128,2048]{1,0:T(8,128)(2,1)S(1)} fusion(f32[128,2048]{1,0:T(8,128)} %get-tuple-element.8, f32[128]{0:T(128)S(1)} %get-tuple-element.4, f32[128]{0:T(128)S(1)} %convert_element_type.36), kind=kLoop, calls=%fused_computation.9 | loop fusion | flops 786432 | bytes 1573888 | tf_op jit(solution)/shard_map/convert_element_type | solution.py:31
  62.4 0.0 copy-start.2
  62.4 0.8 copy-done.2
  63.2 2.7 %convolution_convert_fusion = bf16[2048,768]{1,0:T(8,128)(2,1)} fusion(bf16[128,2048]{1,0:T(8,128)(2,1)S(1)} %multiply_convert_fusion.1, bf16[128,768]{1,0:T(8,128)(2,1)S(1)} %all_gather.7), kind=kOutput, calls=%fused_computation.4 | convolution fusion | flops 404226048 | bytes 3866624 | tf_op jit(solution)/shard_map/dot_general | solution.py:34
  65.9 0.0 all-reduce.3.cloned.1.call-update
  65.9 1.2 fusion.4
  67.2 0.6 dynamic_slice.15
  67.7 5.6 %psum.23 = bf16[2048]{0:T(1024)(128)(2,1)S(1)} all-reduce(bf16[2048]{0:T(1024)(128)(2,1)S(1)} %convert_element_type.45), channel_id=1, replica_groups=mesh['groups'=2,'cent'=4,'dp'=2,'sub'=2] {'dp','sub'}, use_global_device_ids=true, to_apply=%region_7.0 | all-reduce | flops 2048 | bytes 8192 | tf_op jit(solution)/shard_map/psum | solution.py:45
  73.4 0.1 convert_add_fusion
  73.5 60.7 %all-reduce.3.cloned.1.call-done = bf16[2048,768]{1,0:T(8,128)(2,1)} async-done(((bf16[2048,768]{1,0:T(8,128)(2,1)}), bf16[2048,768]{1,0:T(8,128)(2,1)}) %all-reduce.3.cloned.1.call-update) | async-done | bytes 3145744 | tf_op jit(solution)/shard_map/psum | solution.py:44
  134.2 1.6 %multiply_reduce_fusion = (f32[512]{0:T(512)S(1)}, f32[512,768]{1,0:T(8,128)S(1)}) fusion(f32[512]{0:T(512)S(1)} %convert_add_fusion, bf16[2048,768]{1,0:T(8,128)(2,1)S(1)} %fusion.1, s32[]{:T(128)S(6)} %select_n.8, bf16[2048,768]{1,0:T(8,128)(2,1)} %all-reduce.3.cloned.1.call-done), kind=kLoop, calls=%fused_computation.7 | loop fusion | flops 2358784 | bytes 3149828 | tf_op jit(solution)/shard_map/reduce_sum | solution.py:9
  135.8 0.0 copy-start.1
  135.8 1.4 multiply_convert_fusion
  137.2 0.0 copy-done.1
  (7 shorter events, 0.0 us)
Async XLA Ops:
  7.2 17.0 %copy-start.3 = (bf16[32,768]{1,0:T(8,128)(2,1)S(1)}, bf16[32,768]{1,0:T(8,128)(2,1)}, u32[]{:S(2)}) copy-start(bf16[32,768]{1,0:T(8,128)(2,1)} %param.4) | copy-start | bytes 147460
  7.2 127.0 %all-reduce.3.cloned.1.call-start = ((), (), s32[]{:S(2)}) async-start(), calls=%async_computation | async-start | bytes 6291456 | tf_op jit(solution)/shard_map/psum | solution.py:44
  21.5 16.4 %copy-start = (bf16[2048,768]{1,0:T(8,128)(2,1)S(1)}, bf16[2048,768]{1,0:T(8,128)(2,1)}, u32[]{:S(2)}) copy-start(bf16[2048,768]{1,0:T(8,128)(2,1)} %param.6) | copy-start | bytes 9437188
  62.4 0.8 copy-start.2
  135.8 1.4 copy-start.1
Sparse Core Ops, SparseCore 0:
  66.0 68.1 all-reduce.2
where the time goes:
time: 145 us; the launch traced here: 144 us
  waiting for transfers between devices  60.8 us (42%)
  blocking collectives  47.9 us (33%)
  between operations  15.4 us (11%)
  other arithmetic  10.4 us (7%)
  matrix products  6.06 us (4%)
  local copies, waits for them, and re-layouts  3.49 us (2%)
    psum x1, waiting for transfers between devices, shards(): lax.psum(partial_value, ('dp', 'sub')).astype(jnp.float32)  60.7 us
    all_gather x1, blocking collectives, shards(): lax.all_gather(unit_rows, 'cent', axis=0, tiled=True)  13.6 us
    pmax x1, blocking collectives, shards(): row_peak = lax.pmax(local_peak, 'cent')  10.4 us
    unnamed x1, blocking collectives  9.89 us
    psum x1, blocking collectives, shards(): lax.psum(jnp.sum(jnp.exp(scores - row_peak[:, None]), axis=1), 'cent')  8.37 us
    psum x1, blocking collectives, shards(): lax.psum(weight_mass, ('dp', 'sub')).astype(jnp.float32)  5.64 us
    reduce_sum x3, other arithmetic, normalize(): jnp.sum(floats * floats, axis=-1, keepdims=True) + 1e-06  5.22 us
    unnamed x11, local copies, waits for them, and re-layouts  2.9 us
  transfers between devices with their start and end apart: 1, of which 1 were waited for; matrix products, arithmetic and copies ran while one was open for 1% of the time, Pallas kernels for 0%

commit v1 on v0

--- a/solution.py
+++ b/solution.py
@@ -41,7 +41,7 @@
     own_count = centroids.shape[0] // lax.axis_size(("dp", "sub"))
     offset = lax.axis_index(("dp", "sub")) * own_count
     panel_sums, panel_mass = (
-        lax.psum(partial_value, ("dp", "sub")).astype(jnp.float32),
+        lax.psum(lax.psum(partial_value, "sub"), "dp").astype(jnp.float32),
         lax.psum(weight_mass, ("dp", "sub")).astype(jnp.float32),
     )
     centroid_sums = lax.dynamic_slice_in_dim(panel_sums, offset, own_count, 0)

time: 145 us -> 189 us (1.30)
  waiting for transfers between devices: 60.8 us -> 103 us
    psum x1 -> x2, waiting for transfers between devices: 60.7 us -> 103 us  [the longest x1 80.2 us: shards(): lax.psum(lax.psum(partial_value, 'sub'), 'dp').astype(jnp.float32)]
  transfers between devices with their start and end apart: 1 -> 2, of which waited for: 1 -> 2; matrix products, arithmetic and copies ran while one was open for 1% -> 1% of each run, Pallas kernels for 0% -> 0%
where the time goes in v1:
time: 189 us; the launch traced here: 188 us
  waiting for transfers between devices  103 us (54%)
  blocking collectives  49.5 us (26%)
  between operations  15.4 us (8%)
  other arithmetic  10.4 us (6%)
  matrix products  6.06 us (3%)
  local copies, waits for them, and re-layouts  3.49 us (2%)
    psum x1, waiting for transfers between devices, shards(): lax.psum(lax.psum(partial_value, 'sub'), 'dp').astype(jnp.float32)  80.2 us
    psum x1, waiting for transfers between devices, shards(): lax.psum(partial_value, 'sub')  23 us
    all_gather x1, blocking collectives, shards(): lax.all_gather(unit_rows, 'cent', axis=0, tiled=True)  13.6 us
    pmax x1, blocking collectives, shards(): row_peak = lax.pmax(local_peak, 'cent')  10.4 us
    unnamed x1, blocking collectives  9.89 us
    psum x1, blocking collectives, shards(): lax.psum(jnp.sum(jnp.exp(scores - row_peak[:, None]), axis=1), 'cent')  8.37 us
    psum x1, blocking collectives, shards(): lax.psum(weight_mass, ('dp', 'sub')).astype(jnp.float32)  7.26 us
    reduce_sum x3, other arithmetic, normalize(): jnp.sum(floats * floats, axis=-1, keepdims=True) + 1e-06  5.22 us
  transfers between devices with their start and end apart: 2, of which 2 were waited for; matrix products, arithmetic and copies ran while one was open for 1% of the time, Pallas kernels for 0%

profile of v1, /device:TPU:0, one launch (start us, length us, event | category | flops | bytes accessed | tf_op | source)
XLA Modules:
  0.0 188.1 jit_solution(1024910235909614288)
XLA Ops:
  7.2 0.0 copy-start.3
  7.2 0.0 all-reduce.4.cloned.1.call-start
  7.9 0.9 fusion.2
  8.8 1.2 dynamic-slice
  10.7 0.9 dynamic-update-slice
  11.6 9.9 %all-reduce = s32[128]{0:T(128)S(1)} all-reduce(s32[128]{0:T(128)S(1)} %dynamic-update-slice), channel_id=1, replica_groups=mesh['groups'=2,'cent'=4,'dp'=2,'sub'=2] {'cent'}, use_global_device_ids=true, to_apply=%add | all-reduce | flops 128 | bytes 1024
  21.5 0.0 copy-start
  21.5 2.7 %fusion = f32[2048]{0:T(1024)S(1)} fusion(bf16[2048,768]{1,0:T(8,128)(2,1)} %param.6), kind=kLoop, calls=%fused_computation.2 | loop fusion | flops 4716544 | bytes 3153920 | tf_op jit(solution)/shard_map/reduce_sum | solution.py:9
  24.2 0.0 copy-done.3
  24.2 0.1 fusion.3
  24.3 13.6 %all_gather.7 = bf16[128,768]{1,0:T(8,128)(2,1)S(1)} all-gather(bf16[32,768]{1,0:T(8,128)(2,1)S(1)} %fusion.3), channel_id=1, replica_groups=mesh['groups'=2,'cent'=4,'dp'=2,'sub'=2] {'cent'}, dimensions={0}, use_global_device_ids=true | all-gather | bytes 245760 | tf_op jit(solution)/shard_map/all_gather | solution.py:17
  37.9 0.0 copy-done
  37.9 0.6 fusion.1
  38.4 2.1 %fusion.7 = (f32[128]{0:T(128)S(1)}, f32[128,2048]{1,0:T(8,128)}) fusion(f32[]{:T(128)} %bitcast.8, bf16[128,768]{1,0:T(8,128)(2,1)S(1)} %all_gather.7, bf16[2048,768]{1,0:T(8,128)(2,1)S(1)} %fusion.1), kind=kOutput, calls=%fused_computation.25 | convolution fusion | flops 403177344 | bytes 4391428 | tf_op jit(solution)/shard_map/dot_general | solution.py:21
  40.6 10.4 %pmax.7 = f32[128]{0:T(128)S(1)} all-reduce(f32[128]{0:T(128)S(1)} %get-tuple-element.7), channel_id=1, replica_groups=mesh['groups'=2,'cent'=4,'dp'=2,'sub'=2] {'cent'}, use_global_device_ids=true, to_apply=%region_3.0 | all-reduce | flops 128 | bytes 1024 | tf_op jit(solution)/shard_map/pmax | solution.py:27
  51.0 1.5 exponential_reduce_fusion
  52.5 8.4 %psum.28 = f32[128]{0:T(128)S(1)} all-reduce(f32[128]{0:T(128)S(1)} %exponential_reduce_fusion), channel_id=1, replica_groups=mesh['groups'=2,'cent'=4,'dp'=2,'sub'=2] {'cent'}, use_global_device_ids=true, to_apply=%region_5.0 | all-reduce | flops 128 | bytes 1024 | tf_op jit(solution)/shard_map/psum | solution.py:28
  60.9 1.5 multiply_convert_fusion.1
  62.4 0.0 copy-start.2
  62.4 0.8 copy-done.2
  63.2 2.7 %convolution_convert_fusion = bf16[2048,768]{1,0:T(8,128)(2,1)} fusion(bf16[128,2048]{1,0:T(8,128)(2,1)S(1)} %multiply_convert_fusion.1, bf16[128,768]{1,0:T(8,128)(2,1)S(1)} %all_gather.7), kind=kOutput, calls=%fused_computation.4 | convolution fusion | flops 404226048 | bytes 3866624 | tf_op jit(solution)/shard_map/dot_general | solution.py:34
  65.9 0.0 all-reduce.4.cloned.1.call-update
  65.9 0.0 all-reduce.6.cloned.1.call-start
  66.0 23.0 %all-reduce.4.cloned.1.call-done = bf16[2048,768]{1,0:T(8,128)(2,1)} async-done(((bf16[2048,768]{1,0:T(8,128)(2,1)}), bf16[2048,768]{1,0:T(8,128)(2,1)}) %all-reduce.4.cloned.1.call-update) | async-done | bytes 3145744 | tf_op jit(solution)/shard_map/psum | solution.py:44
  88.9 0.0 all-reduce.6.cloned.1.call-update
  89.0 1.2 fusion.4
  90.2 0.6 dynamic_slice.15
  90.8 7.3 %psum.31 = bf16[2048]{0:T(1024)(128)(2,1)S(1)} all-reduce(bf16[2048]{0:T(1024)(128)(2,1)S(1)} %convert_element_type.45), channel_id=1, replica_groups=mesh['groups'=2,'cent'=4,'dp'=2,'sub'=2] {'dp','sub'}, use_global_device_ids=true, to_apply=%region_8.0 | all-reduce | flops 2048 | bytes 8192 | tf_op jit(solution)/shard_map/psum | solution.py:45
  98.1 0.1 convert_add_fusion
  98.1 80.2 %all-reduce.6.cloned.1.call-done = bf16[2048,768]{1,0:T(8,128)(2,1)} async-done(((bf16[2048,768]{1,0:T(8,128)(2,1)}), bf16[2048,768]{1,0:T(8,128)(2,1)}) %all-reduce.6.cloned.1.call-update) | async-done | bytes 3145744 | tf_op jit(solution)/shard_map/psum | solution.py:44
  178.3 1.6 multiply_reduce_fusion
  179.9 0.0 copy-start.1
  179.9 1.4 multiply_convert_fusion
  181.3 0.0 copy-done.1
  (7 shorter events, 0.0 us)
Async XLA Ops:
  7.2 17.0 %copy-start.3 = (bf16[32,768]{1,0:T(8,128)(2,1)S(1)}, bf16[32,768]{1,0:T(8,128)(2,1)}, u32[]{:S(2)}) copy-start(bf16[32,768]{1,0:T(8,128)(2,1)} %param.4) | copy-start | bytes 147460
  7.2 81.8 %all-reduce.4.cloned.1.call-start = ((), (), s32[]{:S(2)}) async-start(), calls=%async_computation | async-start | bytes 6291456 | tf_op jit(solution)/shard_map/psum | solution.py:44
  21.5 16.4 %copy-start = (bf16[2048,768]{1,0:T(8,128)(2,1)S(1)}, bf16[2048,768]{1,0:T(8,128)(2,1)}, u32[]{:S(2)}) copy-start(bf16[2048,768]{1,0:T(8,128)(2,1)} %param.6) | copy-start | bytes 9437188
  62.4 0.8 copy-start.2
  65.9 112.4 %all-reduce.6.cloned.1.call-start = ((), (), s32[]{:S(2)}) async-start(), calls=%async_computation.1 | async-start | bytes 6291456 | tf_op jit(solution)/shard_map/psum | solution.py:44
  179.9 1.4 copy-start.1
Sparse Core Ops, SparseCore 0:
  66.0 22.8 all-reduce.3
  91.3 86.9 all-reduce.5
